TPU v7x, 512 devices: a whole 4x8x8 slice. The times are simulated.
512 devices in a mesh: gx: 32 (over x, z), gy: 16 (over y, core).
Axes of the slice: x: 4, y: 8, z: 8, core: 2. Of those that a mesh axis runs over, the one named last changes fastest.
Arguments:
- sources: float32 [1024, 512, 192], P('gx', 'gy'), may hold values from -12 to 12
- permeability: float32 [1024, 512], P('gx', 'gy'), may hold values from 0.2 to 5
- storage: float32 [1024, 512], P('gx', 'gy'), may hold values from 0.05 to 1
- basis: float32 [8, 1024, 512], P(None, 'gx', 'gy'), may hold values from -0.3 to 0.3
- local_inverse: bfloat16 [32, 16, 1024, 1600], P('gx', 'gy'), may hold values from -0.2 to 0.4
- coarse_inverse: float32 [4096, 4096], P(('gx', 'gy')), may hold values from -1.2 to 2.2
Outputs:
- solution: float32 [1024, 512, 192], P('gx', 'gy')
- residual_norms: float32 [3, 192], replicated
- initial_norms: float32 [192], replicated
All inputs are finite; a program needn't handle non-finite values.
Results may differ from a plain program's by a relative error of at most 0.0007.
Values may be sent and summed in bfloat16 or wider, within the bound.
No kernel may reach another device: no remote copies, remote signals or barrier semaphores. Data moves between devices by JAX's collectives and lax.ppermute only.
A program may use at most 64 MiB of HBM per device.

v0:
```python
import jax
import jax.numpy as jnp
from jax import lax
from jax.sharding import PartitionSpec as P

OV = 4
ITERS = 3
lower_bound = 0.15
upper_bound = 1.9
highest = lax.Precision.HIGHEST


def extended(cells, sides, width):
    for axis, dim in sides:
        count = lax.axis_size(axis)
        ends = count - 1
        head = lax.slice_in_dim(cells, 0, width, axis=dim)
        tail = lax.slice_in_dim(cells, cells.shape[dim] - width, cells.shape[dim], axis=dim)
        cells = jnp.concatenate(
            [
                lax.ppermute(tail, axis, [(i, (i + 1) % count) for i in range(ends)]),
                cells,
                lax.ppermute(head, axis, [((i + 1) % count, i) for i in range(ends)]),
            ],
            axis=dim,
        )
    return cells


def neighbour(padded, offset_row, offset_col):
    inner_rows = padded.shape[0] - 2
    inner_cols = padded.shape[1] - 2
    return padded[
        1 + offset_row : 1 + offset_row + inner_rows, 1 + offset_col : 1 + offset_col + inner_cols
    ]


def operate(field_pad, kappa_pad, storage_used):
    centre = neighbour(field_pad, 0, 0)
    kappa = neighbour(kappa_pad, 0, 0)
    total = storage_used[:, :, None] * centre
    for offset_row, offset_col in ((1, 0), (-1, 0), (0, 1), (0, -1)):
        faces = 0.5 * (kappa + neighbour(kappa_pad, offset_row, offset_col))
        total = total + faces[:, :, None] * (centre - neighbour(field_pad, offset_row, offset_col))
    return total


def on_device(sources, permeability, storage, basis, local_inverse, coarse_inverse):
    patch = sources.shape[0]
    fields = sources.shape[2]
    modes = basis.shape[0]
    margin = OV
    extent = patch + 2 * margin
    cells = float(patch * patch * lax.axis_size("gx") * lax.axis_size("gy"))
    flat_basis = basis.reshape(modes, patch * patch)
    inverse_rows = local_inverse[0, 0]
    stacked = jnp.stack([permeability, storage])
    padded = extended(stacked, (("gx", 1), ("gy", 2)), 1)
    kappa_pad = padded[0]
    state = sources

    def rounded_window(current):
        return extended(current.astype(jnp.bfloat16), (("gx", 0), ("gy", 1)), margin)

    def squares_total(current_core):
        return lax.psum(jnp.sum(current_core * current_core, axis=(0, 1)), ("gx", "gy"))

    def precondition(current):
        window = rounded_window(current).reshape(extent * extent, fields)
        local_part = jnp.dot(inverse_rows, window, preferred_element_type=jnp.float32).reshape(
            patch, patch, fields
        )
        flat_core = current.reshape(patch * patch, fields)
        restricted = jnp.dot(flat_basis, flat_core, precision=highest)
        coarse_part = jnp.dot(
            coarse_inverse,
            lax.all_gather(restricted, ("gx", "gy"), axis=0, tiled=True),
            precision=highest,
        )
        squares = squares_total(current)
        prolonged = jnp.dot(flat_basis.T, coarse_part, precision=highest).reshape(
            patch, patch, fields
        )
        return (local_part + prolonged, squares)

    centre = 0.5 * (upper_bound + lower_bound)
    half_width = 0.5 * (upper_bound - lower_bound)
    relative = centre / half_width
    weight_prev = 1.0 / relative
    solution = jnp.zeros_like(sources)
    corrected, initial = precondition(state)
    history = []
    update = corrected / centre
    for index in range(ITERS):
        solution = solution + update
        step_pad = extended(update, (("gx", 0), ("gy", 1)), 1)
        state = state - operate(step_pad, kappa_pad, storage)
        if index + 1 < ITERS:
            corrected, squares = precondition(state)
            history.append(squares)
            weight_next = 1.0 / (2.0 * relative - weight_prev)
            update = weight_next * weight_prev * update + 2.0 * weight_next / half_width * corrected
            weight_prev = weight_next
        else:
            history.append(squares_total(state))
    return (solution, jnp.sqrt(jnp.stack(history) / cells), jnp.sqrt(initial / cells))


def solution(mesh):
    placed = (
        P("gx", "gy", None),
        P("gx", "gy"),
        P("gx", "gy"),
        P(None, "gx", "gy"),
        P("gx", "gy", None, None),
        P(("gx", "gy"), None),
    )
    return jax.shard_map(
        on_device,
        mesh=mesh,
        in_specs=placed,
        out_specs=(P("gx", "gy", None), P(), P()),
        check_vma=False,
    )
```

profile of v0, /device:TPU:1, one launch (start us, length us, event | category | flops | bytes accessed | tf_op | source)
XLA Modules:
  0.0 572.1 jit_solution(11102322538769110874)
XLA Ops:
  7.2 2.8 convolution_bitcast_fusion.2
  11.5 5.4 collective-permute-start.4
  22.0 4.7 collective-permute-start
  33.1 5.6 collective-permute-start.2
  41.9 3.1 collective-permute-start.6
  49.4 86.9 %all-gather.4.cloned.1.call-done = f32[4096,192]{1,0:T(8,128)} async-done(((f32[8,192]{1,0:T(8,128)}), f32[4096,192]{1,0:T(8,128)}) %all-gather.4.cloned.1.call-update) | async-done | bytes 3145744 | tf_op jit(solution)/shard_map/all_gather | solution.py:77
  136.3 4.3 fusion.90
  147.2 2.7 collective-permute-start.9
  152.1 2.5 collective-permute-done.8
  154.7 3.6 collective-permute-start.10
  161.6 2.5 multiply_reduce_fusion.2
  167.7 3.1 collective-permute-start.12
  172.5 4.0 collective-permute-done.13
  176.5 5.0 collective-permute-start.14
  183.7 4.0 collective-permute-done.15
  189.1 96.9 %all-gather.6.cloned.1.call-done = f32[4096,192]{1,0:T(8,128)} async-done(((f32[8,192]{1,0:T(8,128)}), f32[4096,192]{1,0:T(8,128)}) %all-gather.6.cloned.1.call-update) | async-done | bytes 3145744 | tf_op jit(solution)/shard_map/all_gather | solution.py:77
  285.9 4.3 fusion.92
  297.2 2.7 collective-permute-start.17
  301.2 3.3 collective-permute-done.16
  304.6 3.6 collective-permute-start.18
  311.6 2.6 fusion.81
  317.3 3.1 collective-permute-start.20
  322.1 3.9 collective-permute-done.21
  327.0 5.1 collective-permute-start.22
  334.1 4.0 collective-permute-done.23
  340.4 95.6 %all-gather.8.cloned.1.call-done = f32[4096,192]{1,0:T(8,128)} async-done(((f32[8,192]{1,0:T(8,128)}), f32[4096,192]{1,0:T(8,128)}) %all-gather.8.cloned.1.call-update) | async-done | bytes 3145744 | tf_op jit(solution)/shard_map/all_gather | solution.py:77
  436.0 4.3 fusion.94
  445.4 3.3 multiply_add_fusion
  448.8 2.8 collective-permute-start.25
  452.9 3.3 collective-permute-done.24
  456.3 3.6 collective-permute-start.26
  465.3 99.0 %all-reduce = (f32[1,192]{1,0:T(1,128)S(1)}, f32[1,192]{1,0:T(1,128)S(1)}, f32[1,192]{1,0:T(1,128)S(1)}, f32[192]{0:T(256)S(1)}) all-reduce(f32[1,192]{1,0:T(1,128)S(1)} %bitcast.86, f32[1,192]{1,0:T(1,128)S(1)} %bitcast.85, f32[1,192]{1,0:T(1,128)S(1)} %bitcast.87, f32[192]{0:T(256)S(1)} %copy-done.32), channel_id=1, replica_groups=mesh['gx'=32,'gy'=16] {'gx','gy'}, use_global_device_ids=true, to_apply=%region_5.0 | all-reduce | flops 768 | bytes 6144 | tf_op jit(solution)/shard_map/psum | solution.py:66
  (149 shorter events, 76.0 us)
Async XLA Ops:
  7.2 134.2 %copy-start = (bf16[1,1,1024,1600]{2,3,1,0:T(8,128)(2,1)S(1)}, bf16[1,1,1024,1600]{2,3,1,0:T(8,128)(2,1)}, u32[]{:S(2)}) copy-start(bf16[1,1,1024,1600]{2,3,1,0:T(8,128)(2,1)} %param.10) | copy-start | bytes 9830404
  7.2 129.1 %all-gather.4.cloned.1.call-start = ((), (), s32[]{:S(2)}) async-start(), calls=%async_computation | async-start | bytes 4202496 | tf_op jit(solution)/shard_map/all_gather | solution.py:77
  10.1 275.8 %all-gather.6.cloned.1.call-start = ((), (), s32[]{:S(2)}) async-start(), calls=%async_computation.1 | async-start | bytes 4202496 | tf_op jit(solution)/shard_map/all_gather | solution.py:77
  11.5 17.8 %collective-permute-start.4 = (f32[2,1,32]{2,1,0:T(1,128)}, f32[2,1,32]{2,1,0:T(1,128)}, u32[]{:S(2)}, u32[]{:S(2)}) collective-permute-start(f32[2,1,32]{2,1,0:T(1,128)} %get-tuple-element.43), channel_id=1, source_target_pairs={{0,16},{16,32},{32,48},{48,64},{64,80},{80,96},{96,112},{112,128},... | collective-permute-start | bytes 776 | tf_op jit(solution)/shard_map/ppermute | solution.py:21
  16.8 12.5 %collective-permute-start.5 = (f32[2,1,32]{2,1,0:T(1,128)}, f32[2,1,32]{2,1,0:T(1,128)}, u32[]{:S(2)}, u32[]{:S(2)}) collective-permute-start(f32[2,1,32]{2,1,0:T(1,128)} %get-tuple-element.44), channel_id=1, source_target_pairs={{16,0},{32,16},{48,32},{64,48},{80,64},{96,80},{112,96},{128,112},... | collective-permute-start | bytes 776 | tf_op jit(solution)/shard_map/ppermute | solution.py:23
  22.0 8.1 %collective-permute-start = (bf16[4,32,192]{2,1,0:T(8,128)(2,1)}, bf16[4,32,192]{2,1,0:T(8,128)(2,1)}, u32[]{:S(2)}, u32[]{:S(2)}) collective-permute-start(bf16[4,32,192]{2,1,0:T(8,128)(2,1)} %get-tuple-element.39), channel_id=1, source_target_pairs={{0,16},{16,32},{32,48},{48,64},{64,80},{80,96},{96,112},{112,128},... | collective-permute-start | bytes 147464 | tf_op jit(solution)/shard_map/ppermute | solution.py:21
  26.7 5.3 collective-permute-start.1
  33.1 13.8 %collective-permute-start.2 = (bf16[40,4,192]{2,1,0:T(4,128)(2,1)S(1)}, bf16[40,4,192]{2,1,0:T(4,128)(2,1)S(1)}, u32[]{:S(2)}, u32[]{:S(2)}) collective-permute-start(bf16[40,4,192]{2,1,0:T(4,128)(2,1)S(1)} %get-tuple-element.33), channel_id=1, source_target_pairs={{0,1},{1,2},{2,3},{3,4},{4,5},{5,6},{6,7},{7,8},{8,9},{9,10},{10,1... | collective-permute-start | bytes 184328 | tf_op jit(solution)/shard_map/ppermute | solution.py:21
  38.7 8.2 %collective-permute-start.3 = (bf16[40,4,192]{2,1,0:T(4,128)(2,1)S(1)}, bf16[40,4,192]{2,1,0:T(4,128)(2,1)S(1)}, u32[]{:S(2)}, u32[]{:S(2)}) collective-permute-start(bf16[40,4,192]{2,1,0:T(4,128)(2,1)S(1)} %get-tuple-element.34), channel_id=1, source_target_pairs={{1,0},{2,1},{3,2},{4,3},{5,4},{6,5},{7,6},{8,7},{9,8},{10,9},{11,1... | collective-permute-start | bytes 184328 | tf_op jit(solution)/shard_map/ppermute | solution.py:23
  41.9 109.3 %collective-permute-start.6 = (f32[2,34,1]{2,1,0:T(8,128)}, f32[2,34,1]{2,1,0:T(8,128)}, u32[]{:S(2)}, u32[]{:S(2)}) collective-permute-start(f32[2,34,1]{2,1,0:T(8,128)} %get-tuple-element.41), channel_id=1, source_target_pairs={{0,1},{1,2},{2,3},{3,4},{4,5},{5,6},{6,7},{7,8},{8,9},{9,10},{10,1... | collective-permute-start | bytes 824 | tf_op jit(solution)/shard_map/ppermute | solution.py:21
  45.0 106.2 %collective-permute-start.7 = (f32[2,34,1]{2,1,0:T(8,128)}, f32[2,34,1]{2,1,0:T(8,128)}, u32[]{:S(2)}, u32[]{:S(2)}) collective-permute-start(f32[2,34,1]{2,1,0:T(8,128)} %get-tuple-element.42), channel_id=1, source_target_pairs={{1,0},{2,1},{3,2},{4,3},{5,4},{6,5},{7,6},{8,7},{9,8},{10,9},{11,1... | collective-permute-start | bytes 824 | tf_op jit(solution)/shard_map/ppermute | solution.py:23
  147.2 4.9 collective-permute-start.9
  149.9 4.7 collective-permute-start.8
  154.7 6.0 %collective-permute-start.10 = (f32[34,1,192]{2,1,0:T(1,128)S(1)}, f32[34,1,192]{2,1,0:T(1,128)S(1)}, u32[]{:S(2)}, u32[]{:S(2)}) collective-permute-start(f32[34,1,192]{2,1,0:T(1,128)S(1)} %get-tuple-element.19), channel_id=1, source_target_pairs={{1,0},{2,1},{3,2},{4,3},{5,4},{6,5},{7,6},{8,7},{9,8},{10,9},{11,1... | collective-permute-start | bytes 78344 | tf_op jit(solution)/shard_map/ppermute | solution.py:23
  158.3 3.3 collective-permute-start.11
  166.4 269.6 %all-gather.8.cloned.1.call-start = ((), (), s32[]{:S(2)}) async-start(), calls=%async_computation.2 | async-start | bytes 4202496 | tf_op jit(solution)/shard_map/all_gather | solution.py:77
  167.7 4.7 collective-permute-start.12
  170.8 5.6 collective-permute-start.13
  176.5 7.2 %collective-permute-start.14 = (bf16[40,4,192]{2,1,0:T(4,128)(2,1)S(1)}, bf16[40,4,192]{2,1,0:T(4,128)(2,1)S(1)}, u32[]{:S(2)}, u32[]{:S(2)}) collective-permute-start(bf16[40,4,192]{2,1,0:T(4,128)(2,1)S(1)} %get-tuple-element.31), channel_id=1, source_target_pairs={{0,1},{1,2},{2,3},{3,4},{4,5},{5,6},{6,7},{7,8},{8,9},{9,10},{10,1... | collective-permute-start | bytes 184328 | tf_op jit(solution)/shard_map/ppermute | solution.py:21
  181.6 6.2 %collective-permute-start.15 = (bf16[40,4,192]{2,1,0:T(4,128)(2,1)S(1)}, bf16[40,4,192]{2,1,0:T(4,128)(2,1)S(1)}, u32[]{:S(2)}, u32[]{:S(2)}) collective-permute-start(bf16[40,4,192]{2,1,0:T(4,128)(2,1)S(1)} %get-tuple-element.32), channel_id=1, source_target_pairs={{1,0},{2,1},{3,2},{4,3},{5,4},{6,5},{7,6},{8,7},{9,8},{10,9},{11,1... | collective-permute-start | bytes 184328 | tf_op jit(solution)/shard_map/ppermute | solution.py:23
  297.2 4.0 collective-permute-start.17
  299.9 4.7 collective-permute-start.16
  304.6 5.9 %collective-permute-start.18 = (f32[34,1,192]{2,1,0:T(1,128)S(1)}, f32[34,1,192]{2,1,0:T(1,128)S(1)}, u32[]{:S(2)}, u32[]{:S(2)}) collective-permute-start(f32[34,1,192]{2,1,0:T(1,128)S(1)} %get-tuple-element.17), channel_id=1, source_target_pairs={{1,0},{2,1},{3,2},{4,3},{5,4},{6,5},{7,6},{8,7},{9,8},{10,9},{11,1... | collective-permute-start | bytes 78344 | tf_op jit(solution)/shard_map/ppermute | solution.py:23
  308.3 3.3 collective-permute-start.19
  317.3 4.8 collective-permute-start.20
  320.4 5.6 collective-permute-start.21
  327.0 7.0 %collective-permute-start.22 = (bf16[40,4,192]{2,1,0:T(4,128)(2,1)S(1)}, bf16[40,4,192]{2,1,0:T(4,128)(2,1)S(1)}, u32[]{:S(2)}, u32[]{:S(2)}) collective-permute-start(bf16[40,4,192]{2,1,0:T(4,128)(2,1)S(1)} %get-tuple-element.29), channel_id=1, source_target_pairs={{0,1},{1,2},{2,3},{3,4},{4,5},{5,6},{6,7},{7,8},{8,9},{9,10},{10,1... | collective-permute-start | bytes 184328 | tf_op jit(solution)/shard_map/ppermute | solution.py:21
  332.1 5.9 %collective-permute-start.23 = (bf16[40,4,192]{2,1,0:T(4,128)(2,1)S(1)}, bf16[40,4,192]{2,1,0:T(4,128)(2,1)S(1)}, u32[]{:S(2)}, u32[]{:S(2)}) collective-permute-start(bf16[40,4,192]{2,1,0:T(4,128)(2,1)S(1)} %get-tuple-element.30), channel_id=1, source_target_pairs={{1,0},{2,1},{3,2},{4,3},{5,4},{6,5},{7,6},{8,7},{9,8},{10,9},{11,1... | collective-permute-start | bytes 184328 | tf_op jit(solution)/shard_map/ppermute | solution.py:23
  448.8 4.2 collective-permute-start.25
  451.6 4.7 collective-permute-start.24
  456.3 5.9 %collective-permute-start.26 = (f32[34,1,192]{2,1,0:T(1,128)S(1)}, f32[34,1,192]{2,1,0:T(1,128)S(1)}, u32[]{:S(2)}, u32[]{:S(2)}) collective-permute-start(f32[34,1,192]{2,1,0:T(1,128)S(1)} %get-tuple-element.15), channel_id=1, source_target_pairs={{1,0},{2,1},{3,2},{4,3},{5,4},{6,5},{7,6},{8,7},{9,8},{10,9},{11,1... | collective-permute-start | bytes 78344 | tf_op jit(solution)/shard_map/ppermute | solution.py:23
  460.0 3.3 collective-permute-start.27
  (33 other events, 562.9 us)
Sparse Core Ops, SparseCore 0:
  12.2 124.0 all-gather.3
  166.5 119.3 all-gather.5
  316.6 119.3 all-gather.7
where the time goes:
time: 574 us; the launch traced here: 572 us
  waiting for transfers between devices  310 us (54%)
  blocking collectives  99 us (17%)
  starting transfers between devices  78.5 us (14%)
  other arithmetic  30.5 us (5%)
  matrix products  26.2 us (5%)
  between operations  14.4 us (3%)
  local copies, waits for them, and re-layouts  13.3 us (2%)
    all_gather x3, waiting for transfers between devices, precondition(): lax.all_gather(restricted, ('gx', 'gy'), axis=0, tiled=True)  279 us
    psum x1, blocking collectives, squares_total(): lax.psum(jnp.sum(current_core * current_core, axis=(0, 1)), ('gx', 'gy'))  99 us
    ppermute x14, starting transfers between devices, extended(): lax.ppermute(tail, axis, [(i, (i + 1) % count) for i in range(ends)])  50.1 us
    ppermute x14, starting transfers between devices, extended(): lax.ppermute(head, axis, [((i + 1) % count, i) for i in range(ends)])  28.3 us
    ppermute x14, waiting for transfers between devices, extended(): lax.ppermute(head, axis, [((i + 1) % count, i) for i in range(ends)])  27 us
    dot_general x3, matrix products, precondition(): jnp.dot(coarse_inverse, lax.all_gather(restricted, ('gx', 'gy'), axis=0,...  12.9 us
  transfers between devices with their start and end apart: 31, of which 16 were waited for; matrix products, arithmetic and copies ran while one was open for 5% of the time, Pallas kernels for 0%

commit v1 on v0

--- a/solution.py
+++ b/solution.py
@@ -8,6 +8,11 @@
 lower_bound = 0.15
 upper_bound = 1.9
 highest = lax.Precision.HIGHEST
+
+
+def expand_grid(base_x, a_name):
+    tile_out = lax.all_gather(base_x, a_name).sum(axis=0)
+    return tile_out
 
 
 def extended(cells, sides, width):
@@ -63,7 +68,7 @@
         return extended(current.astype(jnp.bfloat16), (("gx", 0), ("gy", 1)), margin)
 
     def squares_total(current_core):
-        return lax.psum(jnp.sum(current_core * current_core, axis=(0, 1)), ("gx", "gy"))
+        return expand_grid(jnp.sum(current_core * current_core, axis=(0, 1)), ("gx", "gy"))
 
     def precondition(current):
         window = rounded_window(current).reshape(extent * extent, fields)

time: 574 us -> 781 us (1.36)
  waiting for transfers between devices: 310 us -> 584 us
  blocking collectives: 99 us -> 0 us
  local copies, waits for them, and re-layouts: 13.3 us -> 29.9 us
  starting transfers between devices: 78.5 us -> 87.2 us
    unnamed x3 -> x5, waiting for transfers between devices: 0.05 us -> 282 us
    psum x1 -> x0, blocking collectives: 99 us -> none  [squares_total(): lax.psum(jnp.sum(current_core * current_core, axis=(0, 1)), ('gx', 'gy'))]
    ppermute x14, waiting for transfers between devices: 27 us -> 6.71 us  [extended(): lax.ppermute(head, axis, [((i + 1) % count, i) for i in range(ends)])]
    unnamed x68 -> x78, local copies, waits for them, and re-layouts: 2.93 us -> 11.7 us
    all_gather x3, waiting for transfers between devices: 279 us -> 288 us  [precondition(): lax.all_gather(restricted, ('gx', 'gy'), axis=0, tiled=True)]
  transfers between devices with their start and end apart: 31 -> 32, of which waited for: 16 -> 14; matrix products, arithmetic and copies ran while one was open for 5% -> 4% of each run, Pallas kernels for 0% -> 0%
where the time goes in v1:
time: 781 us; the launch traced here: 779 us
  waiting for transfers between devices  584 us (75%)
  starting transfers between devices  87.2 us (11%)
  other arithmetic  37.1 us (5%)
  local copies, waits for them, and re-layouts  29.9 us (4%)
  matrix products  26.1 us (3%)
  between operations  14.5 us (2%)
    all_gather x3, waiting for transfers between devices, precondition(): lax.all_gather(restricted, ('gx', 'gy'), axis=0, tiled=True)  288 us
    unnamed x5, waiting for transfers between devices  282 us
    ppermute x14, starting transfers between devices, extended(): lax.ppermute(tail, axis, [(i, (i + 1) % count) for i in range(ends)])  57.3 us
    ppermute x14, starting transfers between devices, extended(): lax.ppermute(head, axis, [((i + 1) % count, i) for i in range(ends)])  29.7 us
  transfers between devices with their start and end apart: 32, of which 14 were waited for; matrix products, arithmetic and copies ran while one was open for 4% of the time, Pallas kernels for 0%

profile of v1, /device:TPU:1, one launch (start us, length us, event | category | flops | bytes accessed | tf_op | source)
XLA Modules:
  0.0 778.6 jit_solution(11953575737199568472)
XLA Ops:
  7.2 2.8 convolution_bitcast_fusion.2
  15.3 6.1 collective-permute-start
  23.2 4.6 collective-permute-start.4
  30.9 8.4 %collective-permute-start.3 = (bf16[40,4,192]{2,1,0:T(4,128)(2,1)S(1)}, bf16[40,4,192]{2,1,0:T(4,128)(2,1)S(1)}, u32[]{:S(2)}, u32[]{:S(2)}) collective-permute-start(bf16[40,4,192]{2,1,0:T(4,128)(2,1)S(1)} %get-tuple-element.34), channel_id=1, source_target_pairs={{1,0},{2,1},{3,2},{4,3},{5,4},{6,5},{7,6},{8,7},{9,8},{10,9},{11,1... | collective-permute-start | bytes 184328 | tf_op jit(solution)/shard_map/ppermute | solution.py:28
  41.9 2.4 collective-permute-start.7
  44.3 3.2 collective-permute-start.6
  49.9 86.4 %all-gather.8.cloned.1.call-done = f32[4096,192]{1,0:T(8,128)} async-done(((f32[8,192]{1,0:T(8,128)}), f32[4096,192]{1,0:T(8,128)}) %all-gather.8.cloned.1.call-update) | async-done | bytes 3145744 | tf_op jit(solution)/shard_map/all_gather | solution.py:82
  136.3 4.3 fusion.90
  143.2 2.5 copy.18
  148.5 4.0 collective-permute-start.9
  153.6 4.3 collective-permute-start.11
  160.0 3.2 collective-permute-done.10
  163.2 2.5 multiply_reduce_fusion.2
  170.6 4.6 collective-permute-start.12
  178.5 3.8 collective-permute-start.14
  185.0 101.6 %all-gather.10.cloned.1.call-done = f32[4096,192]{1,0:T(8,128)} async-done(((f32[8,192]{1,0:T(8,128)}), f32[4096,192]{1,0:T(8,128)}) %all-gather.10.cloned.1.call-update) | async-done | bytes 3145744 | tf_op jit(solution)/shard_map/all_gather | solution.py:82
  286.5 4.3 fusion.92
  293.5 2.5 copy.20
  299.1 4.0 collective-permute-start.17
  304.2 4.3 collective-permute-start.19
  310.5 3.3 collective-permute-done.18
  313.8 2.6 fusion.81
  320.9 4.6 collective-permute-start.20
  329.8 3.6 collective-permute-start.22
  337.3 100.0 %all-gather.12.cloned.1.call-done = f32[4096,192]{1,0:T(8,128)} async-done(((f32[8,192]{1,0:T(8,128)}), f32[4096,192]{1,0:T(8,128)}) %all-gather.12.cloned.1.call-update) | async-done | bytes 3145744 | tf_op jit(solution)/shard_map/all_gather | solution.py:82
  437.3 4.3 fusion.94
  444.2 2.4 copy.22
  446.7 3.3 multiply_add_fusion
  451.4 4.0 collective-permute-start.25
  456.5 4.3 collective-permute-start.27
  467.5 4.9 multiply_reduce_fusion.1
  476.9 281.8 %all-reduce.7.cloned.1.call-done = (f32[98304]{0:T(1024)}, f32[98304]{0:T(1024)}, f32[98304]{0:T(1024)}, f32[98304]{0:T(1024)}) async-done(((f32[98304]{0:T(1024)}, f32[98304]{0:T(1024)}, f32[98304]{0:T(1024)}, f32[98304]{0:T(1024)}), (f32[98304]{0:T(1024)}, f32[98304]{0:T(1024)}, f32[98304]{0:T(1024)}, f32[98304]{0:T(1024)})) %all-reduce.7.cloned.1.call-update) | async-done | bytes 1572880
  (169 shorter events, 85.4 us)
Async XLA Ops:
  7.2 129.1 %all-gather.8.cloned.1.call-start = ((), (), s32[]{:S(2)}) async-start(), calls=%async_computation | async-start | bytes 4202496 | tf_op jit(solution)/shard_map/all_gather | solution.py:82
  10.1 276.5 %all-gather.10.cloned.1.call-start = ((), (), s32[]{:S(2)}) async-start(), calls=%async_computation.1 | async-start | bytes 4202496 | tf_op jit(solution)/shard_map/all_gather | solution.py:82
  14.0 15.9 %collective-permute-start.1 = (bf16[4,32,192]{2,1,0:T(8,128)(2,1)}, bf16[4,32,192]{2,1,0:T(8,128)(2,1)}, u32[]{:S(2)}, u32[]{:S(2)}) collective-permute-start(bf16[4,32,192]{2,1,0:T(8,128)(2,1)} %get-tuple-element.40), channel_id=1, source_target_pairs={{16,0},{32,16},{48,32},{64,48},{80,64},{96,80},{112,96},{128,112},... | collective-permute-start | bytes 147464 | tf_op jit(solution)/shard_map/ppermute | solution.py:28
  15.3 14.6 %collective-permute-start = (bf16[4,32,192]{2,1,0:T(8,128)(2,1)}, bf16[4,32,192]{2,1,0:T(8,128)(2,1)}, u32[]{:S(2)}, u32[]{:S(2)}) collective-permute-start(bf16[4,32,192]{2,1,0:T(8,128)(2,1)} %get-tuple-element.39), channel_id=1, source_target_pairs={{0,16},{16,32},{32,48},{48,64},{64,80},{80,96},{96,112},{112,128},... | collective-permute-start | bytes 147464 | tf_op jit(solution)/shard_map/ppermute | solution.py:26
  21.9 7.2 collective-permute-start.5
  23.2 5.9 collective-permute-start.4
  30.9 16.6 %collective-permute-start.3 = (bf16[40,4,192]{2,1,0:T(4,128)(2,1)S(1)}, bf16[40,4,192]{2,1,0:T(4,128)(2,1)S(1)}, u32[]{:S(2)}, u32[]{:S(2)}) collective-permute-start(bf16[40,4,192]{2,1,0:T(4,128)(2,1)S(1)} %get-tuple-element.34), channel_id=1, source_target_pairs={{1,0},{2,1},{3,2},{4,3},{5,4},{6,5},{7,6},{8,7},{9,8},{10,9},{11,1... | collective-permute-start | bytes 184328 | tf_op jit(solution)/shard_map/ppermute | solution.py:28
  39.3 8.2 %collective-permute-start.2 = (bf16[40,4,192]{2,1,0:T(4,128)(2,1)S(1)}, bf16[40,4,192]{2,1,0:T(4,128)(2,1)S(1)}, u32[]{:S(2)}, u32[]{:S(2)}) collective-permute-start(bf16[40,4,192]{2,1,0:T(4,128)(2,1)S(1)} %get-tuple-element.33), channel_id=1, source_target_pairs={{0,1},{1,2},{2,3},{3,4},{4,5},{5,6},{6,7},{7,8},{8,9},{9,10},{10,1... | collective-permute-start | bytes 184328 | tf_op jit(solution)/shard_map/ppermute | solution.py:26
  41.9 110.6 %collective-permute-start.7 = (f32[2,34,1]{2,1,0:T(8,128)}, f32[2,34,1]{2,1,0:T(8,128)}, u32[]{:S(2)}, u32[]{:S(2)}) collective-permute-start(f32[2,34,1]{2,1,0:T(8,128)} %get-tuple-element.42), channel_id=1, source_target_pairs={{1,0},{2,1},{3,2},{4,3},{5,4},{6,5},{7,6},{8,7},{9,8},{10,9},{11,1... | collective-permute-start | bytes 824 | tf_op jit(solution)/shard_map/ppermute | solution.py:28
  44.3 108.2 %collective-permute-start.6 = (f32[2,34,1]{2,1,0:T(8,128)}, f32[2,34,1]{2,1,0:T(8,128)}, u32[]{:S(2)}, u32[]{:S(2)}) collective-permute-start(f32[2,34,1]{2,1,0:T(8,128)} %get-tuple-element.41), channel_id=1, source_target_pairs={{0,1},{1,2},{2,3},{3,4},{4,5},{5,6},{6,7},{7,8},{8,9},{9,10},{10,1... | collective-permute-start | bytes 824 | tf_op jit(solution)/shard_map/ppermute | solution.py:26
  147.2 6.2 collective-permute-start.8
  148.5 5.0 collective-permute-start.9
  153.6 6.4 collective-permute-start.11
  157.9 5.3 collective-permute-start.10
  168.0 269.3 %all-gather.12.cloned.1.call-start = ((), (), s32[]{:S(2)}) async-start(), calls=%async_computation.2 | async-start | bytes 4202496 | tf_op jit(solution)/shard_map/all_gather | solution.py:82
  169.3 5.9 collective-permute-start.13
  170.6 5.9 collective-permute-start.12
  176.6 5.8 collective-permute-start.15
  178.5 5.1 collective-permute-start.14
  297.8 5.3 collective-permute-start.16
  299.1 5.0 collective-permute-start.17
  304.2 6.3 collective-permute-start.19
  308.6 5.3 collective-permute-start.18
  318.7 439.9 %all-reduce.7.cloned.1.call-start = ((), (), s32[]{:S(2)}) async-start(), calls=%async_computation.3 | async-start | bytes 3145728
  319.6 5.9 collective-permute-start.21
  320.9 5.9 collective-permute-start.20
  327.9 5.8 collective-permute-start.23
  329.8 5.1 collective-permute-start.22
  450.0 5.4 collective-permute-start.24
  451.4 5.0 collective-permute-start.25
  456.5 10.9 %collective-permute-start.27 = (f32[34,1,192]{2,1,0:T(1,128)S(1)}, f32[34,1,192]{2,1,0:T(1,128)S(1)}, u32[]{:S(2)}, u32[]{:S(2)}) collective-permute-start(f32[34,1,192]{2,1,0:T(1,128)S(1)} %get-tuple-element.16), channel_id=1, source_target_pairs={{0,1},{1,2},{2,3},{3,4},{4,5},{5,6},{6,7},{7,8},{8,9},{9,10},{10,1... | collective-permute-start | bytes 78344 | tf_op jit(solution)/shard_map/ppermute | solution.py:26
  460.8 6.6 collective-permute-start.26
  (35 other events, 731.8 us)
Sparse Core Ops, SparseCore 0:
  12.2 124.0 all-gather.7
  168.1 118.4 all-gather.9
  318.8 118.4 all-gather.11
  477.0 281.5 all-reduce.6
